TPU v7x, 128 devices: a whole 4x4x4 slice. The times are simulated.
128 devices in a mesh: seq: 32 (over x, y, core), fsdp: 4 (over z).
Axes of the slice: x: 4, y: 4, z: 4, core: 2. Of those that a mesh axis runs over, the one named last changes fastest.
Arguments:
- patches: bfloat16 [32768, 1280], P(('seq', 'fsdp')), may hold values from -6 to 6
- vis_index: int32 [32768], P(('seq', 'fsdp')), may hold values from 0 to 131071, as said below
- kv_list: int32 [256, 16], P(('seq', 'fsdp')), may hold values from 0 to 255, as said below
- kv_count: int32 [256], P(('seq', 'fsdp')), may hold values from 1 to 16, as said below
- global_tiles: int32 [2], replicated, may hold values from 0 to 255
- frame_table: bfloat16 [256, 1280], replicated, may hold values from -3 to 3
- space_table: bfloat16 [512, 1280], replicated, may hold values from -3 to 3
- ln_gain: bfloat16 [1280], replicated, may hold values from 0.25 to 1.75
- ln_bias: bfloat16 [1280], replicated, may hold values from -3 to 3
- w_qkv: bfloat16 [1280, 3840], P('fsdp')
- w_out: bfloat16 [1280, 1280], P('fsdp'), may hold values from -1.25 to 1.25
Outputs:
- attended: bfloat16 [32768, 1280], P(('seq', 'fsdp'))
Inputs may be any that keep to these rules, and one draw needn't show every extreme that they name: `vis_index`: exactly one visible position in each aligned group of four; strictly increasing. `kv_list`: the first entry of query tile i is i itself; entries may repeat; every entry t satisfies |t // 8 - i // 8| <= 2. Over all entries of an aligned run of 2 query tiles, the tiles that lie in any one group other than the run's own group (group = tile // 8) number at most 3 distinct ones, and exactly 3 for every such group within two of the run's own. On every device at least one query tile has kv_count = 16.
All inputs are finite; a program needn't handle non-finite values.
Results may differ from a plain program's by a relative error of at most 0.0065.
Values may be sent and summed in bfloat16 or wider, within the bound.
No kernel may reach another device: no remote copies, remote signals or barrier semaphores. Data moves between devices by JAX's collectives and lax.ppermute only.
A program may use at most 192 MiB of HBM per device.

v0:
```python
import jax
import jax.numpy as jnp
from jax import lax
from jax.sharding import PartitionSpec as P

HEADS = 16
TILE = 128
KT = 16
GLOBAL = 2
PATCHES = 512
NEAR = 3
REACH = (-2, -1, 1, 2)


def passed_along(block, axis, distance):
    devices = range(lax.axis_size(axis))
    route = [(i - distance, i) for i in devices if i - distance in devices]
    return lax.ppermute(block, axis, route)


def layer_norm(stream, ln_gain, ln_bias):
    stream32 = stream.astype(jnp.float32)
    mean_val = jnp.mean(stream32, axis=-1, keepdims=True)
    centred = stream32 - mean_val
    variance = jnp.mean(centred * centred, axis=-1, keepdims=True)
    scaled = centred * lax.rsqrt(variance + 1e-06)
    return (scaled * ln_gain.astype(jnp.float32) + ln_bias.astype(jnp.float32)).astype(jnp.bfloat16)


def embed(patches, vis_index, frame_table, space_table):
    frame_ids = vis_index // PATCHES
    patch_ids = vis_index % PATCHES
    return (
        patches.astype(jnp.float32)
        + frame_table[frame_ids].astype(jnp.float32)
        + space_table[patch_ids].astype(jnp.float32)
    ).astype(jnp.bfloat16)


def near_tiles(entries, group, group_tiles):
    cand = group * group_tiles + jnp.arange(group_tiles, dtype=jnp.int32)
    named = jnp.any(entries.reshape(-1, 1) == cand[None, :], axis=0)
    rank = jnp.cumsum(named.astype(jnp.int32)) - 1
    local_ids = jnp.arange(group_tiles, dtype=jnp.int32)
    picks = jnp.stack([jnp.sum(jnp.where(named & (rank == j), local_ids, 0)) for j in range(NEAR)])
    return (picks, rank)


def attend_tile(query_tile, key_values, key_live, feat_width):
    head_size = feat_width // HEADS
    key_rows = key_values.shape[0]
    queries_h = query_tile.reshape(TILE, HEADS, head_size)
    keys_h = key_values[:, :feat_width].reshape(key_rows, HEADS, head_size)
    values_h = key_values[:, feat_width:].reshape(key_rows, HEADS, head_size)
    scores = jnp.einsum(
        "qhd,khd->hqk", queries_h, keys_h, preferred_element_type=jnp.float32
    ) * head_size ** (-0.5)
    scores = jnp.where(key_live[None, None, :], scores, -jnp.inf)
    row_max = jnp.max(scores, axis=-1, keepdims=True)
    weights_raw = jnp.exp(scores - row_max)
    probs = (weights_raw / jnp.sum(weights_raw, axis=-1, keepdims=True)).astype(jnp.bfloat16)
    mixed_h = jnp.einsum("hqk,khd->qhd", probs, values_h, preferred_element_type=jnp.float32)
    return mixed_h.reshape(TILE, feat_width).astype(jnp.bfloat16)


def local(
    patches,
    vis_index,
    kv_list,
    kv_count,
    global_tiles,
    frame_table,
    space_table,
    ln_gain,
    ln_bias,
    w_qkv,
    w_out,
):
    tok_rows = patches.shape[0]
    feat_width = patches.shape[1]
    tile_count = tok_rows // TILE
    fsdp_size = lax.axis_size("fsdp")
    seq_size = lax.axis_size("seq")
    seq_at = lax.axis_index("seq")
    dev_at = seq_at * fsdp_size + lax.axis_index("fsdp")
    group_tiles = tile_count * fsdp_size
    stream = embed(patches, vis_index, frame_table, space_table)
    global_rows = []
    for slot_no in range(GLOBAL):
        tile_id = global_tiles[slot_no]
        mine = tile_id // tile_count == dev_at
        rows = lax.dynamic_slice_in_dim(stream, tile_id % tile_count * TILE, TILE, 0)
        global_rows.append(jnp.where(mine, rows, jnp.zeros_like(rows)))
    global_stream = lax.psum(jnp.concatenate(global_rows, axis=0), ("seq", "fsdp"))
    w_full = lax.all_gather(w_qkv, "fsdp", axis=0, tiled=True)
    normed = layer_norm(stream, ln_gain, ln_bias)
    qkv = jnp.dot(normed, w_full, preferred_element_type=jnp.float32).astype(jnp.bfloat16)
    query = qkv[:, :feat_width]
    keyval = qkv[:, feat_width:]
    global_normed = layer_norm(global_stream, ln_gain, ln_bias)
    global_kv = (
        jnp.dot(global_normed, w_full[:, feat_width:], preferred_element_type=jnp.float32)
        .astype(jnp.bfloat16)
        .reshape(GLOBAL, TILE, 2 * feat_width)
    )
    group_block = lax.all_gather(keyval, "fsdp", axis=0, tiled=True).reshape(
        group_tiles, TILE, 2 * feat_width
    )
    seq_lists = lax.all_gather(kv_list, "seq", axis=0, tiled=True)
    near_blocks = []
    near_rank = []
    for reach in REACH:
        distance = -reach
        dest = jnp.clip(seq_at + distance, 0, seq_size - 1)
        dest_lists = lax.dynamic_slice_in_dim(seq_lists, dest * tile_count, tile_count, 0)
        send_ids, unused = near_tiles(dest_lists, seq_at, group_tiles)
        sent = passed_along(group_block[send_ids], "seq", distance)
        near_blocks.append(sent)
        unused2, rank = near_tiles(kv_list, seq_at + reach, group_tiles)
        near_rank.append(rank)
    window = jnp.concatenate([group_block] + near_blocks + [global_kv], axis=0)
    near_rank = jnp.stack(near_rank)
    entry_group = kv_list // group_tiles
    entry_local = kv_list % group_tiles
    reach_of = entry_group - seq_at
    reach_slot = jnp.where(reach_of < 0, reach_of + 2, reach_of + 1)
    reach_slot = jnp.clip(reach_slot, 0, len(REACH) - 1)
    entry_rank = near_rank[reach_slot, entry_local]
    local_lists = jnp.where(
        reach_of == 0, entry_local, group_tiles + NEAR * reach_slot + entry_rank
    )
    global_slots = group_tiles + NEAR * len(REACH) + jnp.arange(GLOBAL, dtype=jnp.int32)
    query_tiles = query.reshape(tile_count, TILE, feat_width)

    def per_tile(tile_args):
        query_tile, local_ids, live_count = tile_args
        slot_live_row = jnp.concatenate(
            [jnp.arange(KT) < live_count, jnp.ones((GLOBAL,), dtype=bool)]
        )
        key_live = jnp.repeat(slot_live_row, TILE)
        key_values = window[jnp.concatenate([local_ids, global_slots])].reshape(
            (KT + GLOBAL) * TILE, 2 * feat_width
        )
        return attend_tile(query_tile, key_values, key_live, feat_width)

    heads_out = lax.map(per_tile, (query_tiles, local_lists, kv_count)).reshape(
        tok_rows, feat_width
    )
    return jnp.dot(
        heads_out,
        lax.all_gather(w_out, "fsdp", axis=0, tiled=True),
        preferred_element_type=jnp.float32,
    ).astype(jnp.bfloat16)


def solution(mesh):
    return jax.shard_map(
        local,
        mesh=mesh,
        in_specs=(
            P(("seq", "fsdp"), None),
            P(("seq", "fsdp")),
            P(("seq", "fsdp"), None),
            P(("seq", "fsdp")),
            P(),
            P(),
            P(),
            P(),
            P(),
            P("fsdp", None),
            P("fsdp", None),
        ),
        out_specs=P(("seq", "fsdp"), None),
        check_vma=False,
    )
```

profile of v0, /device:TPU:28, one launch (start us, length us, event | category | flops | bytes accessed | tf_op | source)
XLA Modules:
  0.0 548.4 jit_solution(2590682510310247328)
XLA Ops:
  7.4 0.7 all-gather.5.cloned.1.call-update
  8.1 0.7 convert_element_type.181
  8.8 0.7 convert_element_type.182
  9.5 0.7 compare_select_fusion.2
  10.2 1.3 gather_fusion.2
  11.5 1.2 gather_fusion.3
  12.8 0.4 convert_reduce_fusion.1
  13.1 0.3 fusion.28
  13.5 93.8 %all-gather.5.cloned.1.call-done = bf16[1280,3840]{1,0:T(8,128)(2,1)} async-done(((bf16[320,3840]{1,0:T(8,128)(2,1)}), bf16[1280,3840]{1,0:T(8,128)(2,1)}) %all-gather.5.cloned.1.call-update) | async-done | bytes 9830416 | tf_op jit(solution)/shard_map/all_gather | solution.py:95
  107.2 6.6 %convolution_convert_fusion = bf16[256,3840]{1,0:T(8,128)(2,1)S(1)} fusion(bf16[1280,3840]{1,0:T(8,128)(2,1)} %all-gather.5.cloned.1.call-done, bf16[256,1280]{1,0:T(8,128)(2,1)S(1)} %get-tuple-element.114, f32[1280]{0:T(1024)S(1)} %convert_element_type.182, f32[1280]{0:T(1024)S(1)} %convert_element_type.181, f32[256]{0:T(256)S(1)} %add_rsqrt_fusion.1, ...), kind=kOutput, calls=%fused_computation.34 | convolution fusion | flops 2519531520 | bytes 12464128 | tf_op jit(solution)/shard_map/dot_general | solution.py:97
  113.9 1.2 copy-done.4
  115.2 1.2 slice.46
  116.4 0.6 fusion.80
  122.4 0.9 pad_maximum_fusion
  123.3 0.7 all-gather.9.cloned.1.call-update
  124.1 22.4 %all-gather = s32[32,2,16]{2,1,0:T(2,128)S(1)} all-gather(s32[1,2,16]{2,1,0:T(2,128)S(1)} %bitcast.181), channel_id=1, replica_groups=mesh['seq'=32,'fsdp'=4] {'seq'}, dimensions={0}, use_global_device_ids=true | all-gather | bytes 4224 | tf_op jit(solution)/shard_map/all_gather | solution.py:109
  146.8 0.2 compare_reduce_fusion
  147.3 0.7 fusion.65
  148.2 0.7 fusion.68
  148.9 3.8 fusion.61
  152.9 0.7 fusion.71
  153.9 0.7 fusion.74
  154.6 3.8 fusion.63
  158.4 0.2 compare_reduce_fusion.7
  159.5 0.8 gather_fusion.1
  160.4 14.5 %all-gather.7.cloned.1.call-done = bf16[1024,2560]{1,0:T(8,128)(2,1)} async-done(((bf16[256,2560]{1,0:T(8,128)(2,1)}), bf16[1024,2560]{1,0:T(8,128)(2,1)}) %all-gather.7.cloned.1.call-update) | async-done | bytes 5242896 | tf_op jit(solution)/shard_map/all_gather | solution.py:106
  174.9 4.6 gather_fusion.4
  179.5 3.0 collective-permute-start
  182.5 137.3 %all-reduce.3.cloned.1.call-done = bf16[256,1280]{1,0:T(8,128)(2,1)} async-done(((bf16[256,1280]{1,0:T(8,128)(2,1)}), bf16[256,1280]{1,0:T(8,128)(2,1)}) %all-reduce.3.cloned.1.call-update) | async-done | bytes 655376 | tf_op jit(solution)/shard_map/psum | solution.py:94
  319.8 1.3 convert_reduce_fusion
  321.2 4.5 gather_fusion.5
  325.7 2.1 collective-permute-start.1
  327.8 0.3 fusion.24
  328.1 4.6 gather_fusion.6
  332.7 3.4 collective-permute-start.2
  336.2 4.7 gather_fusion.7
  340.9 2.6 collective-permute-start.3
  343.5 4.8 fusion.17
  348.4 0.3 constant_dynamic-update-slice_fusion.6
  348.7 1.7 constant_dynamic-update-slice_fusion.5
  350.4 1.6 collective-permute-done.1
  351.9 1.7 constant_dynamic-update-slice_fusion.4
  353.6 19.3 %collective-permute-done.2 = bf16[3,128,2560]{2,1,0:T(8,128)(2,1)} collective-permute-done((bf16[3,128,2560]{2,1,0:T(8,128)(2,1)}, bf16[3,128,2560]{2,1,0:T(8,128)(2,1)}, u32[]{:S(2)}, u32[]{:S(2)}) %collective-permute-start.2) | collective-permute-done | bytes 1966112 | tf_op jit(solution)/shard_map/ppermute | solution.py:18
  373.0 1.7 constant_dynamic-update-slice_fusion.3
  374.7 30.7 %collective-permute-done.3 = bf16[3,128,2560]{2,1,0:T(8,128)(2,1)S(1)} collective-permute-done((bf16[3,128,2560]{2,1,0:T(8,128)(2,1)}, bf16[3,128,2560]{2,1,0:T(8,128)(2,1)S(1)}, u32[]{:S(2)}, u32[]{:S(2)}) %collective-permute-start.3) | collective-permute-done | bytes 1966112 | tf_op jit(solution)/shard_map/ppermute | solution.py:18
  405.6 5.0 copy-done.2
  410.6 126.7 %while.11 = (s32[]{:T(128)}, bf16[2,128,1280]{2,1,0:T(8,128)(2,1)S(1)}, s32[2,16]{1,0:T(2,128)S(1)}, bf16[22,128,2560]{2,1,0:T(8,128)(2,1)}, s32[2]{0:T(128)S(1)...) while((s32[]{:T(128)}, bf16[2,128,1280]{2,1,0:T(8,128)(2,1)S(1)}, ...), condition=%wide.region_36.37_spmd.clone, body=%wide.region_33.36_spmd.clone.sunk | while | flops 1538428160 | bytes 123626584 | solution.py:146
  410.7 11.3 %gather_fusion = bf16[18,128,2560]{2,1,0:T(8,128)(2,1)} fusion(bf16[22,128,2560]{2,1,0:T(8,128)(2,1)} %get-tuple-element.205, s32[1024]{0:T(1024)S(1)} %pad_clamp_fusion.8), kind=kCustom, calls=%fused_computation.clone.clone.1 | custom fusion | bytes 23593032 | tf_op jit(solution)/shard_map/while/body/eval_jaxpr/gather | solution.py:141
  422.0 9.7 %fusion.102 = (bf16[2304,1280]{1,0:T(8,128)(2,1)}, bf16[2304,1280]{1,0:T(8,128)(2,1)}) fusion(bf16[2304,2560]{1,0:T(8,128)(2,1)} %bitcast.166), kind=kLoop, calls=%fused_computation.186.clone.1 | loop fusion | bytes 23592960 | tf_op jit(solution)/shard_map/while/body/eval_jaxpr/slice | solution.py:53
  431.7 8.9 %copy.38 = bf16[2304,1280]{0,1:T(8,128)(2,1)} copy(bf16[2304,1280]{1,0:T(8,128)(2,1)} %get-tuple-element.183) | data formatting | bytes 11796480 | tf_op jit(solution)/shard_map/while
  440.7 0.6 dynamic_slice.54
  441.3 0.6 iota_compare_fusion.2
  442.1 11.3 %fusion.103 = (f32[16,128]{1,0:T(8,128)S(1)}, f32[16,128,2304]{2,1,0:T(8,128)}) fusion(pred[2304]{0:T(1024)(128)(4,1)S(1)} %broadcast_bitcast_fusion.2, bf16[128,16,80]{0,2,1:T(8,128)(2,1)S(1)} %bitcast.176, bf16[2304,16,80]{0,2,1:T(8,128)(2,1)} %bitcast.167), kind=kOutput, calls=%fused_computation.187.clone.1 | convolution fusion | flops 773851392 | bytes 25110784 | tf_op jit(solution)/shard_map/while/body/eval_jaxpr/sub | solution.py:60
  453.4 8.9 %copy.36 = bf16[2304,1280]{0,1:T(8,128)(2,1)} copy(bf16[2304,1280]{1,0:T(8,128)(2,1)} %get-tuple-element.182) | data formatting | bytes 11796480 | tf_op jit(solution)/shard_map/while
  462.2 11.5 %fusion.104 = bf16[16,80,128]{2,1,0:T(8,128)(2,1)S(1)} fusion(bf16[2304,16,80]{0,2,1:T(8,128)(2,1)} %bitcast.168, f32[16,128,2304]{2,1,0:T(8,128)} %get-tuple-element.184, f32[16,128]{1,0:T(8,128)S(1)} %get-tuple-element.185), kind=kOutput, calls=%fused_computation.19.clone.1 | convolution fusion | flops 764575744 | bytes 25108480 | tf_op jit(solution)/shard_map/while/body/eval_jaxpr/hqk,khd->qhd/dot_general | solution.py:62
  474.1 11.3 %gather_fusion = bf16[18,128,2560]{2,1,0:T(8,128)(2,1)} fusion(bf16[22,128,2560]{2,1,0:T(8,128)(2,1)} %get-tuple-element.205, s32[1024]{0:T(1024)S(1)} %pad_clamp_fusion.8), kind=kCustom, calls=%fused_computation.clone.clone.1 | custom fusion | bytes 23593032 | tf_op jit(solution)/shard_map/while/body/eval_jaxpr/gather | solution.py:141
  485.4 9.7 %fusion.102 = (bf16[2304,1280]{1,0:T(8,128)(2,1)}, bf16[2304,1280]{1,0:T(8,128)(2,1)}) fusion(bf16[2304,2560]{1,0:T(8,128)(2,1)} %bitcast.166), kind=kLoop, calls=%fused_computation.186.clone.1 | loop fusion | bytes 23592960 | tf_op jit(solution)/shard_map/while/body/eval_jaxpr/slice | solution.py:53
  495.0 8.9 %copy.38 = bf16[2304,1280]{0,1:T(8,128)(2,1)} copy(bf16[2304,1280]{1,0:T(8,128)(2,1)} %get-tuple-element.183) | data formatting | bytes 11796480 | tf_op jit(solution)/shard_map/while
  504.1 0.6 dynamic_slice.54
  504.7 0.6 iota_compare_fusion.2
  505.5 11.3 %fusion.103 = (f32[16,128]{1,0:T(8,128)S(1)}, f32[16,128,2304]{2,1,0:T(8,128)}) fusion(pred[2304]{0:T(1024)(128)(4,1)S(1)} %broadcast_bitcast_fusion.2, bf16[128,16,80]{0,2,1:T(8,128)(2,1)S(1)} %bitcast.176, bf16[2304,16,80]{0,2,1:T(8,128)(2,1)} %bitcast.167), kind=kOutput, calls=%fused_computation.187.clone.1 | convolution fusion | flops 773851392 | bytes 25110784 | tf_op jit(solution)/shard_map/while/body/eval_jaxpr/sub | solution.py:60
  516.7 8.9 %copy.36 = bf16[2304,1280]{0,1:T(8,128)(2,1)} copy(bf16[2304,1280]{1,0:T(8,128)(2,1)} %get-tuple-element.182) | data formatting | bytes 11796480 | tf_op jit(solution)/shard_map/while
  525.6 11.5 %fusion.104 = bf16[16,80,128]{2,1,0:T(8,128)(2,1)S(1)} fusion(bf16[2304,16,80]{0,2,1:T(8,128)(2,1)} %bitcast.168, f32[16,128,2304]{2,1,0:T(8,128)} %get-tuple-element.184, f32[16,128]{1,0:T(8,128)S(1)} %get-tuple-element.185), kind=kOutput, calls=%fused_computation.19.clone.1 | convolution fusion | flops 764575744 | bytes 25108480 | tf_op jit(solution)/shard_map/while/body/eval_jaxpr/hqk,khd->qhd/dot_general | solution.py:62
  537.4 3.9 convolution_convert_fusion.1
  (100 shorter events, 4.1 us)
Async XLA Ops:
  7.4 4.1 copy-start
  7.4 2.8 copy-start.3
  7.4 99.9 %all-gather.5.cloned.1.call-start = ((), (), s32[]{:S(2)}) async-start(), calls=%async_computation | async-start | bytes 12288000 | tf_op jit(solution)/shard_map/all_gather | solution.py:95
  8.1 166.8 %all-gather.7.cloned.1.call-start = ((), (), s32[]{:S(2)}) async-start(), calls=%async_computation.1 | async-start | bytes 6553600 | tf_op jit(solution)/shard_map/all_gather | solution.py:106
  11.5 1.3 copy-start.6
  113.9 1.3 copy-start.4
  115.1 1.2 copy-start.8
  116.3 7.7 %copy-start.7 = (s32[2,16]{1,0:T(2,128)S(1)}, s32[2,16]{1,0:T(2,128)}, u32[]{:S(2)}) copy-start(s32[2,16]{1,0:T(2,128)} %param.15) | copy-start | bytes 388
  116.3 203.5 %all-reduce.3.cloned.1.call-start = ((), (), s32[]{:S(2)}) async-start(), calls=%async_computation.2 | async-start | bytes 1310720 | tf_op jit(solution)/shard_map/psum | solution.py:94
  123.3 414.2 %all-gather.9.cloned.1.call-start = ((), (), s32[]{:S(2)}) async-start(), calls=%async_computation.3 | async-start | bytes 4096000 | tf_op jit(solution)/shard_map/all_gather | solution.py:151
  179.5 169.2 %collective-permute-start = (bf16[3,128,2560]{2,1,0:T(8,128)(2,1)}, bf16[3,128,2560]{2,1,0:T(8,128)(2,1)}, u32[]{:S(2)}, u32[]{:S(2)}) collective-permute-start(bf16[3,128,2560]{2,1,0:T(8,128)(2,1)} %gather_fusion.4), channel_id=1, source_target_pairs={{0,8},{4,12},{8,16},{12,20},{16,24},{20,28},{24,32},{28,36},{32,40... | collective-permute-start | bytes 5898248 | tf_op jit(solution)/shard_map/ppermute | solution.py:18
  319.8 8.0 %copy-start.5 = (bf16[256,1280]{1,0:T(8,128)(2,1)S(1)}, bf16[256,1280]{1,0:T(8,128)(2,1)}, u32[]{:S(2)}) copy-start(bf16[256,1280]{1,0:T(8,128)(2,1)} %all-reduce.3.cloned.1.call-done) | copy-start | bytes 1966084
  325.7 26.3 %collective-permute-start.1 = (bf16[3,128,2560]{2,1,0:T(8,128)(2,1)}, bf16[3,128,2560]{2,1,0:T(8,128)(2,1)}, u32[]{:S(2)}, u32[]{:S(2)}) collective-permute-start(bf16[3,128,2560]{2,1,0:T(8,128)(2,1)} %gather_fusion.5), channel_id=1, source_target_pairs={{0,4},{4,8},{8,12},{12,16},{16,20},{20,24},{24,28},{28,32},{32,36}... | collective-permute-start | bytes 5898248 | tf_op jit(solution)/shard_map/ppermute | solution.py:18
  332.7 40.3 %collective-permute-start.2 = (bf16[3,128,2560]{2,1,0:T(8,128)(2,1)}, bf16[3,128,2560]{2,1,0:T(8,128)(2,1)}, u32[]{:S(2)}, u32[]{:S(2)}) collective-permute-start(bf16[3,128,2560]{2,1,0:T(8,128)(2,1)} %gather_fusion.6), channel_id=1, source_target_pairs={{4,0},{8,4},{12,8},{16,12},{20,16},{24,20},{28,24},{32,28},{36,32}... | collective-permute-start | bytes 5898248 | tf_op jit(solution)/shard_map/ppermute | solution.py:18
  336.2 12.2 %slice-start = ((s8[5242880]{0:T(1024)(128)(4,1)}), s8[1048576]{0:T(1024)(128)(4,1)S(1)}, s32[]{:S(2)}) async-start(s8[5242880]{0:T(1024)(128)(4,1)} %bitcast.173), calls=%async_computation.4 | async-start | bytes 2097152
  340.9 7.5 %slice-start.1 = ((s8[5242880]{0:T(1024)(128)(4,1)}), s8[4194304]{0:T(1024)(128)(4,1)S(1)}, s32[]{:S(2)}) async-start(s8[5242880]{0:T(1024)(128)(4,1)} %bitcast.173), calls=%async_computation.5 | async-start | bytes 8388608
  340.9 64.5 %collective-permute-start.3 = (bf16[3,128,2560]{2,1,0:T(8,128)(2,1)}, bf16[3,128,2560]{2,1,0:T(8,128)(2,1)S(1)}, u32[]{:S(2)}, u32[]{:S(2)}) collective-permute-start(bf16[3,128,2560]{2,1,0:T(8,128)(2,1)} %gather_fusion.7), channel_id=1, source_target_pairs={{8,0},{12,4},{16,8},{20,12},{24,16},{28,20},{32,24},{36,28},{40,32... | collective-permute-start | bytes 5898248 | tf_op jit(solution)/shard_map/ppermute | solution.py:18
  374.6 36.0 %slice-start.2 = ((bf16[256,3840]{1,0:T(8,128)(2,1)}), bf16[256,1280]{1,0:T(8,128)(2,1)S(1)}, s32[]{:S(2)}) async-start(bf16[256,3840]{1,0:T(8,128)(2,1)} %copy-done.4), calls=%async_computation.6 | async-start | bytes 1310720 | tf_op jit(solution)/shard_map/slice | solution.py:98
  374.6 36.0 %copy-start.9 = (s32[2]{0:T(128)S(1)}, s32[2]{0:T(128)}, u32[]{:S(2)}) copy-start(s32[2]{0:T(128)} %param.16) | copy-start | bytes 28
  405.6 5.0 copy-start.2
  537.4 3.9 copy-start.1
Sparse Core Ops, SparseCore 0:
  9.8 97.3 all-gather.4
  116.5 58.4 all-gather.6
  176.6 41.3 all-gather.8
Sparse Core Ops, SparseCore 1:
  123.3 196.4 all-reduce.2
where the time goes:
time: 550 us; the launch traced here: 548 us
  waiting for transfers between devices  299 us (54%)
  local copies, waits for them, and re-layouts  115 us (21%)
  matrix products  61 us (11%)
  blocking collectives  22.4 us (4%)
  between operations  20.2 us (4%)
  other arithmetic  19.5 us (4%)
  starting transfers between devices  11.3 us (2%)
    psum x1, waiting for transfers between devices, local(): lax.psum(jnp.concatenate(global_rows, axis=0), ('seq', 'fsdp'))  137 us
    all_gather x1, waiting for transfers between devices, local(): w_full = lax.all_gather(w_qkv, 'fsdp', axis=0, tiled=True)  93.8 us
    ppermute x4, waiting for transfers between devices, passed_along(): return lax.ppermute(block, axis, route)  51.6 us
    while x4, local copies, waits for them, and re-layouts  35.4 us
    dot_general x2, matrix products, attend_tile(): jnp.einsum('hqk,khd->qhd', probs, values_h, preferred_element_type=jnp.fl...  23.1 us
    sub x2, matrix products, attend_tile(): weights_raw = jnp.exp(scores - row_max)  22.6 us
    gather x2, local copies, waits for them, and re-layouts, per_tile(): window[jnp.concatenate([local_ids, global_slots])]  22.5 us
    all_gather x1, blocking collectives, local(): seq_lists = lax.all_gather(kv_list, 'seq', axis=0, tiled=True)  22.4 us
  transfers between devices with their start and end apart: 8, of which 6 were waited for; matrix products, arithmetic and copies ran while one was open for 32% of the time, Pallas kernels for 0%

commit v1 on v0

--- a/solution.py
+++ b/solution.py
@@ -10,6 +10,22 @@
 PATCHES = 512
 NEAR = 3
 REACH = (-2, -1, 1, 2)
+
+
+def ring_gather(x, axis, dim):
+    ways, here, step = (lax.axis_size(axis), lax.axis_index(axis), x.shape[dim])
+    dims = [n * ways if d == dim else n for d, n in enumerate(x.shape)]
+    full = lax.dynamic_update_slice_in_dim(jnp.zeros(dims, x.dtype), x, here * step, axis=dim)
+    going_up = going_down = x
+    for far in range(1, ways // 2 + 1):
+        going_up = lax.ppermute(going_up, axis, [(d, (d + 1) % ways) for d in range(ways)])
+        full = lax.dynamic_update_slice_in_dim(full, going_up, (here - far) % ways * step, axis=dim)
+        if 2 * far < ways:
+            going_down = lax.ppermute(going_down, axis, [(d, (d - 1) % ways) for d in range(ways)])
+            full = lax.dynamic_update_slice_in_dim(
+                full, going_down, (here + far) % ways * step, axis=dim
+            )
+    return full
 
 
 def passed_along(block, axis, distance):
@@ -103,9 +119,7 @@
         .astype(jnp.bfloat16)
         .reshape(GLOBAL, TILE, 2 * feat_width)
     )
-    group_block = lax.all_gather(keyval, "fsdp", axis=0, tiled=True).reshape(
-        group_tiles, TILE, 2 * feat_width
-    )
+    group_block = ring_gather(keyval, "fsdp", 0).reshape(group_tiles, TILE, 2 * feat_width)
     seq_lists = lax.all_gather(kv_list, "seq", axis=0, tiled=True)
     near_blocks = []
     near_rank = []

time: 550 us -> 502 us (0.913)
  waiting for transfers between devices: 299 us -> 241 us
  local copies, waits for them, and re-layouts: 115 us -> 123 us
    psum x1, waiting for transfers between devices: 137 us -> 57.4 us  [local(): lax.psum(jnp.concatenate(global_rows, axis=0), ('seq', 'fsdp'))]
    ppermute x0 -> x3, waiting for transfers between devices: none -> 68.3 us  [the longest x2 68.3 us: ring_gather(): lax.ppermute(going_up, axis, [(d, (d + 1) % ways) for d in range(ways)])]
    all_gather x1, waiting for transfers between devices: 93.8 us -> 62.4 us  [local(): w_full = lax.all_gather(w_qkv, 'fsdp', axis=0, tiled=True)]
    all_gather x1 -> x0, waiting for transfers between devices: 14.5 us -> none  [local(): lax.all_gather(keyval, 'fsdp', axis=0, tiled=True)]
    dynamic_update_slice x0 -> x3, local copies, waits for them, and re-layouts: none -> 6.13 us  [the longest x2 3.69 us: ring_gather(): lax.dynamic_update_slice_in_dim(full, going_up, (here - far) % ways * ste...]
    unnamed x29 -> x35, local copies, waits for them, and re-layouts: 11.8 us -> 13.7 us
  transfers between devices with their start and end apart: 8 -> 10, of which waited for: 6 -> 7; matrix products, arithmetic and copies ran while one was open for 32% -> 38% of each run, Pallas kernels for 0% -> 0%
where the time goes in v1:
time: 502 us; the launch traced here: 501 us
  waiting for transfers between devices  241 us (48%)
  local copies, waits for them, and re-layouts  123 us (25%)
  matrix products  61.1 us (12%)
  blocking collectives  22.3 us (4%)
  between operations  20.3 us (4%)
  other arithmetic  17.8 us (4%)
  starting transfers between devices  14.4 us (3%)
    ppermute x2, waiting for transfers between devices, ring_gather(): lax.ppermute(going_up, axis, [(d, (d + 1) % ways) for d in range(ways)])  68.3 us
    all_gather x1, waiting for transfers between devices, local(): w_full = lax.all_gather(w_qkv, 'fsdp', axis=0, tiled=True)  62.4 us
    psum x1, waiting for transfers between devices, local(): lax.psum(jnp.concatenate(global_rows, axis=0), ('seq', 'fsdp'))  57.4 us
    ppermute x4, waiting for transfers between devices, passed_along(): return lax.ppermute(block, axis, route)  51.7 us
    while x4, local copies, waits for them, and re-layouts  35.4 us
    dot_general x2, matrix products, attend_tile(): jnp.einsum('hqk,khd->qhd', probs, values_h, preferred_element_type=jnp.fl...  23.1 us
    sub x2, matrix products, attend_tile(): weights_raw = jnp.exp(scores - row_max)  22.6 us
    gather x2, local copies, waits for them, and re-layouts, per_tile(): window[jnp.concatenate([local_ids, global_slots])]  22.5 us
  transfers between devices with their start and end apart: 10, of which 7 were waited for; matrix products, arithmetic and copies ran while one was open for 38% of the time, Pallas kernels for 0%

profile of v1, /device:TPU:28, one launch (start us, length us, event | category | flops | bytes accessed | tf_op | source)
XLA Modules:
  0.0 500.7 jit_solution(375812454244328249)
XLA Ops:
  7.4 0.7 all-gather.4.cloned.1.call-update
  8.1 1.3 fusion.81
  14.4 0.7 compare_select_fusion.2
  15.1 1.3 gather_fusion.2
  16.4 1.2 gather_fusion.3
  17.7 0.4 convert_reduce_fusion.1
  18.2 0.9 pad_maximum_fusion
  19.2 0.7 all-gather.6.cloned.1.call-update
  20.4 22.3 %all-gather = s32[32,2,16]{2,1,0:T(2,128)S(1)} all-gather(s32[1,2,16]{2,1,0:T(2,128)S(1)} %bitcast.181), channel_id=1, replica_groups=mesh['seq'=32,'fsdp'=4] {'seq'}, dimensions={0}, use_global_device_ids=true | all-gather | bytes 4224 | tf_op jit(solution)/shard_map/all_gather | solution.py:123
  43.5 0.7 fusion.65
  45.4 62.4 %all-gather.4.cloned.1.call-done = bf16[1280,3840]{1,0:T(8,128)(2,1)} async-done(((bf16[320,3840]{1,0:T(8,128)(2,1)}), bf16[1280,3840]{1,0:T(8,128)(2,1)}) %all-gather.4.cloned.1.call-update) | async-done | bytes 9830416 | tf_op jit(solution)/shard_map/all_gather | solution.py:111
  107.8 6.7 %convolution_convert_fusion = bf16[256,3840]{1,0:T(8,128)(2,1)S(1)} fusion(bf16[1280,3840]{1,0:T(8,128)(2,1)} %all-gather.4.cloned.1.call-done, bf16[256,1280]{1,0:T(8,128)(2,1)S(1)} %get-tuple-element.114, f32[1280]{0:T(1024)S(1)} %convert_element_type.182, f32[1280]{0:T(1024)S(1)} %convert_element_type.181, f32[256]{0:T(256)S(1)} %add_rsqrt_fusion.1, ...), kind=kOutput, calls=%fused_computation.34 | convolution fusion | flops 2519531520 | bytes 12464128 | tf_op jit(solution)/shard_map/dot_general | solution.py:113
  114.5 0.3 broadcast_in_dim.76
  115.0 0.7 copy-done.5
  115.7 2.4 copy-done.3
  118.1 1.5 collective-permute-start
  119.7 0.7 fusion.68
  120.4 1.8 collective-permute-start.1
  122.2 3.7 fusion.61
  126.4 0.8 gather_fusion.1
  127.2 0.7 fusion.71
  127.9 0.7 fusion.74
  128.6 47.9 %collective-permute-done = bf16[256,2560]{1,0:T(8,128)(2,1)} collective-permute-done((bf16[256,2560]{1,0:T(8,128)(2,1)S(1)}, bf16[256,2560]{1,0:T(8,128)(2,1)}, u32[]{:S(2)}, u32[]{:S(2)}) %collective-permute-start) | collective-permute-done | bytes 1310752 | tf_op jit(solution)/shard_map/ppermute | solution.py:21
  176.5 3.7 fusion.63
  180.2 2.5 constant_dynamic-update-slice_fusion.9
  182.7 2.4 constant_dynamic-update-slice_fusion.8
  185.2 20.4 %collective-permute-done.2 = bf16[256,2560]{1,0:T(8,128)(2,1)S(1)} collective-permute-done((bf16[256,2560]{1,0:T(8,128)(2,1)}, bf16[256,2560]{1,0:T(8,128)(2,1)S(1)}, u32[]{:S(2)}, u32[]{:S(2)}) %collective-permute-start.2) | collective-permute-done | bytes 1310752 | tf_op jit(solution)/shard_map/ppermute | solution.py:21
  205.5 1.2 constant_dynamic-update-slice_fusion.7
  206.8 4.6 gather_fusion.4
  211.3 3.0 collective-permute-start.3
  214.3 57.4 %all-reduce.3.cloned.1.call-done = bf16[256,1280]{1,0:T(8,128)(2,1)} async-done(((bf16[256,1280]{1,0:T(8,128)(2,1)}), bf16[256,1280]{1,0:T(8,128)(2,1)}) %all-reduce.3.cloned.1.call-update) | async-done | bytes 655376 | tf_op jit(solution)/shard_map/psum | solution.py:110
  271.7 1.3 convert_reduce_fusion
  273.1 4.5 gather_fusion.5
  277.6 2.1 collective-permute-start.4
  280.0 4.6 gather_fusion.6
  284.6 3.4 collective-permute-start.5
  288.1 4.7 gather_fusion.7
  292.8 2.5 collective-permute-start.6
  295.3 4.8 fusion.17
  300.5 1.7 constant_dynamic-update-slice_fusion.5
  302.2 1.7 collective-permute-done.4
  303.8 1.7 constant_dynamic-update-slice_fusion.4
  305.5 19.3 %collective-permute-done.5 = bf16[3,128,2560]{2,1,0:T(8,128)(2,1)} collective-permute-done((bf16[3,128,2560]{2,1,0:T(8,128)(2,1)}, bf16[3,128,2560]{2,1,0:T(8,128)(2,1)}, u32[]{:S(2)}, u32[]{:S(2)}) %collective-permute-start.5) | collective-permute-done | bytes 1966112 | tf_op jit(solution)/shard_map/ppermute | solution.py:34
  324.9 1.7 constant_dynamic-update-slice_fusion.3
  326.6 30.6 %collective-permute-done.6 = bf16[3,128,2560]{2,1,0:T(8,128)(2,1)S(1)} collective-permute-done((bf16[3,128,2560]{2,1,0:T(8,128)(2,1)}, bf16[3,128,2560]{2,1,0:T(8,128)(2,1)S(1)}, u32[]{:S(2)}, u32[]{:S(2)}) %collective-permute-start.6) | collective-permute-done | bytes 1966112 | tf_op jit(solution)/shard_map/ppermute | solution.py:34
  357.5 5.0 %copy-done.2 = bf16[22,128,2560]{2,1,0:T(8,128)(2,1)} copy-done((bf16[22,128,2560]{2,1,0:T(8,128)(2,1)}, bf16[22,128,2560]{2,1,0:T(8,128)(2,1)S(1)}, u32[]{:S(2)}) %copy-start.2) | copy-done | bytes 14417944
  362.5 126.8 %while.11 = (s32[]{:T(128)}, bf16[2,128,1280]{2,1,0:T(8,128)(2,1)S(1)}, s32[2,16]{1,0:T(2,128)S(1)}, bf16[22,128,2560]{2,1,0:T(8,128)(2,1)}, s32[2]{0:T(128)S(1)...) while((s32[]{:T(128)}, bf16[2,128,1280]{2,1,0:T(8,128)(2,1)S(1)}, ...), condition=%wide.region_36.37_spmd.clone, body=%wide.region_33.36_spmd.clone.sunk | while | flops 1538428160 | bytes 123626584 | solution.py:160
  362.7 11.3 %gather_fusion = bf16[18,128,2560]{2,1,0:T(8,128)(2,1)} fusion(bf16[22,128,2560]{2,1,0:T(8,128)(2,1)} %get-tuple-element.207, s32[1024]{0:T(1024)S(1)} %pad_clamp_fusion.8), kind=kCustom, calls=%fused_computation.clone.clone.1 | custom fusion | bytes 23593032 | tf_op jit(solution)/shard_map/while/body/eval_jaxpr/gather | solution.py:155
  373.9 9.7 %fusion.103 = (bf16[2304,1280]{1,0:T(8,128)(2,1)}, bf16[2304,1280]{1,0:T(8,128)(2,1)}) fusion(bf16[2304,2560]{1,0:T(8,128)(2,1)} %bitcast.166), kind=kLoop, calls=%fused_computation.190.clone.1 | loop fusion | bytes 23592960 | tf_op jit(solution)/shard_map/while/body/eval_jaxpr/slice | solution.py:69
  383.6 8.9 %copy.38 = bf16[2304,1280]{0,1:T(8,128)(2,1)} copy(bf16[2304,1280]{1,0:T(8,128)(2,1)} %get-tuple-element.185) | data formatting | bytes 11796480 | tf_op jit(solution)/shard_map/while
  392.7 0.6 dynamic_slice.54
  393.3 0.6 iota_compare_fusion.2
  394.0 11.3 %fusion.104 = (f32[16,128]{1,0:T(8,128)S(1)}, f32[16,128,2304]{2,1,0:T(8,128)}) fusion(pred[2304]{0:T(1024)(128)(4,1)S(1)} %broadcast_bitcast_fusion.2, bf16[128,16,80]{0,2,1:T(8,128)(2,1)S(1)} %bitcast.176, bf16[2304,16,80]{0,2,1:T(8,128)(2,1)} %bitcast.167), kind=kOutput, calls=%fused_computation.191.clone.1 | convolution fusion | flops 773851392 | bytes 25110784 | tf_op jit(solution)/shard_map/while/body/eval_jaxpr/sub | solution.py:76
  405.3 8.9 %copy.36 = bf16[2304,1280]{0,1:T(8,128)(2,1)} copy(bf16[2304,1280]{1,0:T(8,128)(2,1)} %get-tuple-element.184) | data formatting | bytes 11796480 | tf_op jit(solution)/shard_map/while
  414.1 11.5 %fusion.105 = bf16[16,80,128]{2,1,0:T(8,128)(2,1)S(1)} fusion(bf16[2304,16,80]{0,2,1:T(8,128)(2,1)} %bitcast.168, f32[16,128,2304]{2,1,0:T(8,128)} %get-tuple-element.186, f32[16,128]{1,0:T(8,128)S(1)} %get-tuple-element.187), kind=kOutput, calls=%fused_computation.19.clone.1 | convolution fusion | flops 764575744 | bytes 25108480 | tf_op jit(solution)/shard_map/while/body/eval_jaxpr/hqk,khd->qhd/dot_general | solution.py:78
  426.0 11.3 %gather_fusion = bf16[18,128,2560]{2,1,0:T(8,128)(2,1)} fusion(bf16[22,128,2560]{2,1,0:T(8,128)(2,1)} %get-tuple-element.207, s32[1024]{0:T(1024)S(1)} %pad_clamp_fusion.8), kind=kCustom, calls=%fused_computation.clone.clone.1 | custom fusion | bytes 23593032 | tf_op jit(solution)/shard_map/while/body/eval_jaxpr/gather | solution.py:155
  437.3 9.7 %fusion.103 = (bf16[2304,1280]{1,0:T(8,128)(2,1)}, bf16[2304,1280]{1,0:T(8,128)(2,1)}) fusion(bf16[2304,2560]{1,0:T(8,128)(2,1)} %bitcast.166), kind=kLoop, calls=%fused_computation.190.clone.1 | loop fusion | bytes 23592960 | tf_op jit(solution)/shard_map/while/body/eval_jaxpr/slice | solution.py:69
  447.0 8.9 %copy.38 = bf16[2304,1280]{0,1:T(8,128)(2,1)} copy(bf16[2304,1280]{1,0:T(8,128)(2,1)} %get-tuple-element.185) | data formatting | bytes 11796480 | tf_op jit(solution)/shard_map/while
  456.1 0.6 dynamic_slice.54
  456.6 0.6 iota_compare_fusion.2
  457.4 11.3 %fusion.104 = (f32[16,128]{1,0:T(8,128)S(1)}, f32[16,128,2304]{2,1,0:T(8,128)}) fusion(pred[2304]{0:T(1024)(128)(4,1)S(1)} %broadcast_bitcast_fusion.2, bf16[128,16,80]{0,2,1:T(8,128)(2,1)S(1)} %bitcast.176, bf16[2304,16,80]{0,2,1:T(8,128)(2,1)} %bitcast.167), kind=kOutput, calls=%fused_computation.191.clone.1 | convolution fusion | flops 773851392 | bytes 25110784 | tf_op jit(solution)/shard_map/while/body/eval_jaxpr/sub | solution.py:76
  468.7 8.9 %copy.36 = bf16[2304,1280]{0,1:T(8,128)(2,1)} copy(bf16[2304,1280]{1,0:T(8,128)(2,1)} %get-tuple-element.184) | data formatting | bytes 11796480 | tf_op jit(solution)/shard_map/while
  477.5 11.5 %fusion.105 = bf16[16,80,128]{2,1,0:T(8,128)(2,1)S(1)} fusion(bf16[2304,16,80]{0,2,1:T(8,128)(2,1)} %bitcast.168, f32[16,128,2304]{2,1,0:T(8,128)} %get-tuple-element.186, f32[16,128]{1,0:T(8,128)S(1)} %get-tuple-element.187), kind=kOutput, calls=%fused_computation.19.clone.1 | convolution fusion | flops 764575744 | bytes 25108480 | tf_op jit(solution)/shard_map/while/body/eval_jaxpr/hqk,khd->qhd/dot_general | solution.py:78
  489.3 3.9 convolution_convert_fusion.1
  (113 shorter events, 5.6 us)
Async XLA Ops:
  7.4 9.0 %copy-start = (bf16[512,1280]{1,0:T(8,128)(2,1)S(1)}, bf16[512,1280]{1,0:T(8,128)(2,1)}, u32[]{:S(2)}) copy-start(bf16[512,1280]{1,0:T(8,128)(2,1)} %param.19) | copy-start | bytes 3932164
  7.4 7.8 %copy-start.4 = (bf16[256,1280]{1,0:T(8,128)(2,1)S(1)}, bf16[256,1280]{1,0:T(8,128)(2,1)}, u32[]{:S(2)}) copy-start(bf16[256,1280]{1,0:T(8,128)(2,1)} %param.18) | copy-start | bytes 1966084
  7.4 100.4 %all-gather.4.cloned.1.call-start = ((), (), s32[]{:S(2)}) async-start(), calls=%async_computation | async-start | bytes 12288000 | tf_op jit(solution)/shard_map/all_gather | solution.py:111
  8.1 263.6 %all-reduce.3.cloned.1.call-start = ((), (), s32[]{:S(2)}) async-start(), calls=%async_computation.1 | async-start | bytes 1310720 | tf_op jit(solution)/shard_map/psum | solution.py:110
  16.4 1.3 copy-start.7
  17.7 2.5 copy-start.9
  17.7 2.6 copy-start.10
  17.7 2.6 copy-start.8
  19.1 470.2 %all-gather.6.cloned.1.call-start = ((), (), s32[]{:S(2)}) async-start(), calls=%async_computation.2 | async-start | bytes 4096000 | tf_op jit(solution)/shard_map/all_gather | solution.py:165
  114.5 1.3 copy-start.5
  115.7 2.4 copy-start.3
  118.1 58.4 %collective-permute-start = (bf16[256,2560]{1,0:T(8,128)(2,1)S(1)}, bf16[256,2560]{1,0:T(8,128)(2,1)}, u32[]{:S(2)}, u32[]{:S(2)}) collective-permute-start(bf16[256,2560]{1,0:T(8,128)(2,1)S(1)} %get-tuple-element.121), channel_id=1, source_target_pairs={{0,1},{1,2},{2,3},{3,0},{4,5},{5,6},{6,7},{7,4},{8,9},{9,10},{10,1... | collective-permute-start | bytes 3932168 | tf_op jit(solution)/shard_map/ppermute | solution.py:21
  120.4 62.3 %collective-permute-start.1 = (bf16[256,2560]{1,0:T(8,128)(2,1)S(1)}, bf16[256,2560]{1,0:T(8,128)(2,1)}, u32[]{:S(2)}, u32[]{:S(2)}) collective-permute-start(bf16[256,2560]{1,0:T(8,128)(2,1)S(1)} %get-tuple-element.121), channel_id=1, source_target_pairs={{0,3},{1,0},{2,1},{3,2},{4,7},{5,4},{6,5},{7,6},{8,11},{9,8},{10,9... | collective-permute-start | bytes 3932168 | tf_op jit(solution)/shard_map/ppermute | solution.py:24
  176.5 29.0 %collective-permute-start.2 = (bf16[256,2560]{1,0:T(8,128)(2,1)}, bf16[256,2560]{1,0:T(8,128)(2,1)S(1)}, u32[]{:S(2)}, u32[]{:S(2)}) collective-permute-start(bf16[256,2560]{1,0:T(8,128)(2,1)} %collective-permute-done), channel_id=1, source_target_pairs={{0,1},{1,2},{2,3},{3,0},{4,5},{5,6},{6,7},{7,4},{8,9},{9,10},{10,1... | collective-permute-start | bytes 3932168 | tf_op jit(solution)/shard_map/ppermute | solution.py:21
  211.3 89.2 %collective-permute-start.3 = (bf16[3,128,2560]{2,1,0:T(8,128)(2,1)}, bf16[3,128,2560]{2,1,0:T(8,128)(2,1)}, u32[]{:S(2)}, u32[]{:S(2)}) collective-permute-start(bf16[3,128,2560]{2,1,0:T(8,128)(2,1)} %gather_fusion.4), channel_id=1, source_target_pairs={{0,8},{4,12},{8,16},{12,20},{16,24},{20,28},{24,32},{28,36},{32,40... | collective-permute-start | bytes 5898248 | tf_op jit(solution)/shard_map/ppermute | solution.py:34
  271.7 8.0 %copy-start.6 = (bf16[256,1280]{1,0:T(8,128)(2,1)S(1)}, bf16[256,1280]{1,0:T(8,128)(2,1)}, u32[]{:S(2)}) copy-start(bf16[256,1280]{1,0:T(8,128)(2,1)} %all-reduce.3.cloned.1.call-done) | copy-start | bytes 1966084
  277.6 26.3 %collective-permute-start.4 = (bf16[3,128,2560]{2,1,0:T(8,128)(2,1)}, bf16[3,128,2560]{2,1,0:T(8,128)(2,1)}, u32[]{:S(2)}, u32[]{:S(2)}) collective-permute-start(bf16[3,128,2560]{2,1,0:T(8,128)(2,1)} %gather_fusion.5), channel_id=1, source_target_pairs={{0,4},{4,8},{8,12},{12,16},{16,20},{20,24},{24,28},{28,32},{32,36}... | collective-permute-start | bytes 5898248 | tf_op jit(solution)/shard_map/ppermute | solution.py:34
  284.6 40.3 %collective-permute-start.5 = (bf16[3,128,2560]{2,1,0:T(8,128)(2,1)}, bf16[3,128,2560]{2,1,0:T(8,128)(2,1)}, u32[]{:S(2)}, u32[]{:S(2)}) collective-permute-start(bf16[3,128,2560]{2,1,0:T(8,128)(2,1)} %gather_fusion.6), channel_id=1, source_target_pairs={{4,0},{8,4},{12,8},{16,12},{20,16},{24,20},{28,24},{32,28},{36,32}... | collective-permute-start | bytes 5898248 | tf_op jit(solution)/shard_map/ppermute | solution.py:34
  288.1 12.0 %slice-start = ((s8[5242880]{0:T(1024)(128)(4,1)}), s8[1048576]{0:T(1024)(128)(4,1)S(1)}, s32[]{:S(2)}) async-start(s8[5242880]{0:T(1024)(128)(4,1)} %bitcast.173), calls=%async_computation.3 | async-start | bytes 2097152
  292.8 7.4 %slice-start.1 = ((s8[5242880]{0:T(1024)(128)(4,1)}), s8[4194304]{0:T(1024)(128)(4,1)S(1)}, s32[]{:S(2)}) async-start(s8[5242880]{0:T(1024)(128)(4,1)} %bitcast.173), calls=%async_computation.4 | async-start | bytes 8388608
  292.8 64.5 %collective-permute-start.6 = (bf16[3,128,2560]{2,1,0:T(8,128)(2,1)}, bf16[3,128,2560]{2,1,0:T(8,128)(2,1)S(1)}, u32[]{:S(2)}, u32[]{:S(2)}) collective-permute-start(bf16[3,128,2560]{2,1,0:T(8,128)(2,1)} %gather_fusion.7), channel_id=1, source_target_pairs={{8,0},{12,4},{16,8},{20,12},{24,16},{28,20},{32,24},{36,28},{40,32... | collective-permute-start | bytes 5898248 | tf_op jit(solution)/shard_map/ppermute | solution.py:34
  326.5 36.0 %slice-start.2 = ((bf16[256,3840]{1,0:T(8,128)(2,1)}), bf16[256,1280]{1,0:T(8,128)(2,1)S(1)}, s32[]{:S(2)}) async-start(bf16[256,3840]{1,0:T(8,128)(2,1)} %copy-done.5), calls=%async_computation.5 | async-start | bytes 1310720 | tf_op jit(solution)/shard_map/slice | solution.py:114
  326.6 36.0 %copy-start.11 = (bf16[2,128,1280]{2,1,0:T(8,128)(2,1)S(1)}, bf16[2,128,1280]{2,1,0:T(8,128)(2,1)}, u32[]{:S(2)}) copy-start(bf16[2,128,1280]{2,1,0:T(8,128)(2,1)} %custom-call.17) | copy-start | bytes 1966084
  326.6 36.0 %copy-start.12 = (s32[2]{0:T(128)S(1)}, s32[2]{0:T(128)}, u32[]{:S(2)}) copy-start(s32[2]{0:T(128)} %param.16) | copy-start | bytes 28
  357.5 5.0 %copy-start.2 = (bf16[22,128,2560]{2,1,0:T(8,128)(2,1)}, bf16[22,128,2560]{2,1,0:T(8,128)(2,1)S(1)}, u32[]{:S(2)}) copy-start(bf16[22,128,2560]{2,1,0:T(8,128)(2,1)S(1)} %constant_dynamic-update-slice_fusion.1) | copy-start | bytes 43253764
  489.3 3.9 copy-start.1
Sparse Core Ops, SparseCore 0:
  9.8 97.8 all-gather.3
  109.4 67.3 all-gather.5
Sparse Core Ops, SparseCore 1:
  19.2 252.5 all-reduce.2
